TPU v7x, 256 devices: a whole 4x4x8 slice. The times are simulated.
256 devices in a mesh: shard: 64 (over x, z_hi, y), rep: 4 (over z_lo, core).
Axes of the slice: x: 4, y: 4, z: 8 (z_hi: 4, z_lo: 2; z = z_hi * 2 + z_lo), core: 2. Of those that a mesh axis runs over, the one named last changes fastest.
Arguments:
- docs: bfloat16 [32768, 16384], P('shard', 'rep')
- pattern: int32 [256, 128], P('shard', 'rep'), may hold values 0 or 1
- owners: int32 [4], replicated, may hold values from 0 to 63
Outputs:
- scores: bfloat16 [4, 256, 32768], P(None, ('shard', 'rep'))
All inputs are finite; a program needn't handle non-finite values. No bound on the sum of `pattern` on one device may be relied on, other than what follows from the above.
Results may differ from a plain program's by a relative error of at most 0.001.
Values may be sent and summed in bfloat16 or wider, within the bound.
No kernel may reach another device: no remote copies, remote signals or barrier semaphores. Data moves between devices by JAX's collectives and lax.ppermute only.
A program may use at most 128 MiB of HBM per device.

v0:
```python
import math
import jax
import jax.numpy as jnp
from jax import lax
from jax.sharding import PartitionSpec as P

TERMS = 16384
QUERY = 256
STEPS = 4
EPSILON = 1e-06
CLIP_LEVEL = 1.5


def from_root(block, axis, owner):
    block = jnp.where(lax.axis_index(axis) == owner, block, jnp.zeros_like(block))
    return lax.psum(block, axis)


def on_device(docs, pattern, owners):
    n_shard = lax.axis_size("shard")
    n_rep = lax.axis_size("rep")
    shard_index = lax.axis_index("shard")
    rep_index = lax.axis_index("rep")
    doc_rows, term_cols = docs.shape
    tile_edge = 128
    row_share = QUERY // (n_shard * n_rep)
    weights = pattern.astype(jnp.bfloat16)
    masked = (
        docs.reshape(doc_rows // tile_edge, tile_edge, term_cols // tile_edge, tile_edge)
        * weights[:, None, :, None]
    ).reshape(doc_rows, term_cols)
    partial_sq = jnp.einsum("dt,dt->d", masked, masked, preferred_element_type=jnp.float32)
    doc_sq = lax.psum(partial_sq, "rep")
    inverse = lax.rsqrt(doc_sq + EPSILON)
    all_inverse = lax.all_gather(inverse, "shard", axis=0, tiled=True)
    sharpen = math.sqrt(TERMS) * 0.5
    results = []
    for step_index in range(STEPS):
        offset = step_index % (doc_rows // QUERY) * QUERY
        candidate = masked[offset : offset + QUERY]
        queries = from_root(candidate, "shard", owners[step_index])
        offset = step_index % (doc_rows // QUERY) * QUERY
        first_global = owners[step_index] * doc_rows + offset
        query_inv = lax.dynamic_slice_in_dim(all_inverse, first_global, QUERY, 0).reshape(
            n_shard, n_rep, row_share
        )
        similar = lax.dot_general(
            queries, masked, (((1,), (1,)), ((), ())), preferred_element_type=jnp.float32
        )
        summed = lax.psum(similar, "rep").reshape(n_shard, n_rep, row_share, doc_rows)
        own_rows = lax.dynamic_index_in_dim(summed, rep_index, 1, keepdims=False)
        received = lax.all_to_all(own_rows, "shard", split_axis=0, concat_axis=2, tiled=True)[0]
        shard_inv = lax.dynamic_index_in_dim(query_inv, shard_index, 0, keepdims=False)
        row_inv = lax.dynamic_index_in_dim(shard_inv, rep_index, 0, keepdims=False)
        scaled = received * row_inv[:, None] * all_inverse[None, :] * sharpen
        results.append(jnp.clip(scaled, -CLIP_LEVEL, CLIP_LEVEL).astype(jnp.bfloat16))
    return jnp.stack(results)


def solution(mesh):
    return jax.shard_map(
        on_device,
        mesh=mesh,
        in_specs=(P("shard", "rep"), P("shard", "rep"), P()),
        out_specs=P(None, ("shard", "rep"), None),
        check_vma=False,
    )
```

profile of v0, /device:TPU:32, one launch (start us, length us, event | category | flops | bytes accessed | tf_op | source)
XLA Modules:
  0.0 1161.1 jit_solution(10522000148827303313)
XLA Ops:
  11.1 3.4 copy.8
  15.5 6.0 copy_bitcast_fusion.2
  21.6 6.0 copy_bitcast_fusion
  28.5 1.6 copy-done
  30.0 3.7 fusion
  33.8 771.8 %all-reduce.7.cloned.1.call-done = (bf16[256,4096]{1,0:T(8,128)(2,1)}, bf16[256,4096]{1,0:T(8,128)(2,1)}, bf16[256,4096]{1,0:T(8,128)(2,1)}, bf16[256,4096]{1,0:T(8,128)(2,1)}) async-done(((bf16[256,4096]{1,0:T(8,128)(2,1)}, bf16[256,4096]{1,0:T(8,128)(2,1)}, bf16[256,4096]{1,0:T(8,128)(2,1)}, bf16[256,4096]{1,0:T(8,128)(2,1)}), (bf16[256,4096]{1,0:T(8,128)(2,1)}, bf16[256,4096]{1,0:T(8,128)(2,1)}, ...) | async-done | bytes 8388624 | tf_op jit(solution)/shard_map/psum | solution.py:16
  805.5 4.2 fusion.3
  810.7 3.8 fusion.4
  815.5 4.3 fusion.5
  820.8 3.8 fusion.6
  825.6 7.8 psum.65
  833.3 52.9 %all-reduce.5.cloned.1.call-done = (f32[64,4,1,512]{3,1,0,2:T(4,128)}, f32[64,4,1,512]{3,1,0,2:T(4,128)}, f32[64,4,1,512]{3,1,0,2:T(4,128)}, f32[64,4,1,512]{3,1,0,2:T(4,128)}) async-done(((f32[64,4,1,512]{3,1,0,2:T(4,128)}, f32[64,4,1,512]{3,1,0,2:T(4,128)}, f32[64,4,1,512]{3,1,0,2:T(4,128)}, f32[64,4,1,512]{3,1,0,2:T(4,128)}), (f32[64,4,1,512]{3,1,0,2:T(4,128)}, f32[64,4,1,512]{3,1,0,2:T(4,128)}, ...) | async-done | bytes 2097168 | tf_op jit(solution)/shard_map/psum | solution.py:50
  886.2 1.8 dynamic-slice_bitcast_fusion.2
  888.0 13.1 %all-to-all-start.1 = ((f32[64,1,512]{2,1,0:T(1,128)}), f32[64,1,512]{2,1,0:T(1,128)S(1)}, u32[]{:S(2)}, u32[]{:S(2)}) async-start(f32[64,1,512]{2,1,0:T(1,128)} %dynamic-slice_bitcast_fusion.2), calls=%async_computation.1 | async-start | bytes 262144 | tf_op jit(solution)/shard_map/all_to_all | solution.py:52
  901.2 1.8 dynamic-slice_bitcast_fusion.1
  903.0 11.3 all-to-all-done.1
  914.3 4.6 all-to-all-start.2
  918.9 192.4 %all-gather = f32[64,1,512]{2,1,0:T(1,128)S(1)} all-gather(f32[1,1,512]{2,1,0:T(1,128)S(1)} %bitcast.81), channel_id=1, replica_groups=mesh['shard'=64,'rep'=4] {'shard'}, dimensions={0}, use_global_device_ids=true | all-gather | bytes 133120 | tf_op jit(solution)/shard_map/all_gather | solution.py:35
  1115.6 1.8 dynamic-slice_bitcast_fusion
  1117.4 4.6 all-to-all-start.3
  1122.1 1.8 dynamic-slice_bitcast_fusion.3
  1124.5 10.1 all-to-all-done.3
  1134.7 4.6 all-to-all-start
  1140.5 11.4 all-to-all-done
  (37 shorter events, 13.7 us)
Async XLA Ops:
  6.5 799.0 %all-reduce.7.cloned.1.call-start = ((), (), s32[]{:S(2)}) async-start(), calls=%async_computation.5 | async-start | bytes 16777216 | tf_op jit(solution)/shard_map/psum | solution.py:16
  27.6 858.6 %all-reduce.5.cloned.1.call-start = ((), (), s32[]{:S(2)}) async-start(), calls=%async_computation.4 | async-start | bytes 4194304 | tf_op jit(solution)/shard_map/psum | solution.py:50
  27.8 2.2 copy-start
  805.5 5.2 copy-start.2
  815.5 5.2 copy-start.1
  888.0 26.2 %all-to-all-start.1 = ((f32[64,1,512]{2,1,0:T(1,128)}), f32[64,1,512]{2,1,0:T(1,128)S(1)}, u32[]{:S(2)}, u32[]{:S(2)}) async-start(f32[64,1,512]{2,1,0:T(1,128)} %dynamic-slice_bitcast_fusion.2), calls=%async_computation.1 | async-start | bytes 262144 | tf_op jit(solution)/shard_map/all_to_all | solution.py:52
  914.3 203.2 %all-to-all-start.2 = ((f32[64,1,512]{2,1,0:T(1,128)}), f32[64,1,512]{2,1,0:T(1,128)S(1)}, u32[]{:S(2)}, u32[]{:S(2)}) async-start(f32[64,1,512]{2,1,0:T(1,128)} %dynamic-slice_bitcast_fusion.1), calls=%async_computation.2 | async-start | bytes 262144 | tf_op jit(solution)/shard_map/all_to_all | solution.py:52
  1117.4 17.2 %all-to-all-start.3 = ((f32[64,1,512]{2,1,0:T(1,128)}), f32[64,1,512]{2,1,0:T(1,128)S(1)}, u32[]{:S(2)}, u32[]{:S(2)}) async-start(f32[64,1,512]{2,1,0:T(1,128)} %dynamic-slice_bitcast_fusion), calls=%async_computation.3 | async-start | bytes 262144 | tf_op jit(solution)/shard_map/all_to_all | solution.py:52
  1134.7 17.2 %all-to-all-start = ((f32[64,1,512]{2,1,0:T(1,128)}), f32[64,1,512]{2,1,0:T(1,128)S(1)}, u32[]{:S(2)}, u32[]{:S(2)}) async-start(f32[64,1,512]{2,1,0:T(1,128)} %dynamic-slice_bitcast_fusion.3), calls=%async_computation | async-start | bytes 262144 | tf_op jit(solution)/shard_map/all_to_all | solution.py:52
Sparse Core Ops, SparseCore 0:
  27.7 777.7 all-reduce.6
  825.7 60.4 all-reduce.4
where the time goes:
time: 1160 us
  waiting for transfers between devices  857 us (74%)
  blocking collectives  200 us (17%)
  local copies, waits for them, and re-layouts  32.3 us (3%)
  starting transfers between devices  27.2 us (2%)
  between operations  18.5 us (2%)
  matrix products  16.1 us (1%)
    psum x1, waiting for transfers between devices, from_root(): return lax.psum(block, axis)  772 us
    all_gather x1, blocking collectives, on_device(): all_inverse = lax.all_gather(inverse, 'shard', axis=0, tiled=True)  192 us
    psum x1, waiting for transfers between devices, on_device(): lax.psum(similar, 'rep').reshape(n_shard, n_rep, row_share, doc_rows)  52.9 us
    all_to_all x4, waiting for transfers between devices, on_device(): lax.all_to_all(own_rows, 'shard', split_axis=0, concat_axis=2, tiled=True)  32.8 us
    all_to_all x4, starting transfers between devices, on_device(): lax.all_to_all(own_rows, 'shard', split_axis=0, concat_axis=2, tiled=True)  27 us
  transfers between devices with their start and end apart: 6, of which 5 were waited for; matrix products, arithmetic and copies ran while one was open for 1% of the time, Pallas kernels for 0%

commit v1 on v0

--- a/solution.py
+++ b/solution.py
@@ -3,6 +3,7 @@
 import jax.numpy as jnp
 from jax import lax
 from jax.sharding import PartitionSpec as P
+from jax.lax import all_gather
 
 TERMS = 16384
 QUERY = 256
@@ -47,7 +48,11 @@
         similar = lax.dot_general(
             queries, masked, (((1,), (1,)), ((), ())), preferred_element_type=jnp.float32
         )
-        summed = lax.psum(similar, "rep").reshape(n_shard, n_rep, row_share, doc_rows)
+
+        def report_the_spots(frame):
+            return all_gather(frame, axis_name="rep").sum(axis=0)
+
+        summed = report_the_spots(similar).reshape(n_shard, n_rep, row_share, doc_rows)
         own_rows = lax.dynamic_index_in_dim(summed, rep_index, 1, keepdims=False)
         received = lax.all_to_all(own_rows, "shard", split_axis=0, concat_axis=2, tiled=True)[0]
         shard_inv = lax.dynamic_index_in_dim(query_inv, shard_index, 0, keepdims=False)

time: 1160 us -> 1140 us (0.983)
  waiting for transfers between devices: 857 us -> 823 us
    psum x1 -> x0, waiting for transfers between devices: 52.9 us -> none  [on_device(): lax.psum(similar, 'rep').reshape(n_shard, n_rep, row_share, doc_rows)]
    all_gather x0 -> x4, waiting for transfers between devices: none -> 28.6 us  [report_the_spots(): return all_gather(frame, axis_name='rep').sum(axis=0)]
  transfers between devices with their start and end apart: 6 -> 9, of which waited for: 5 -> 5; matrix products, arithmetic and copies ran while one was open for 1% -> 3% of each run, Pallas kernels for 0% -> 0%
where the time goes in v1:
time: 1140 us
  waiting for transfers between devices  823 us (72%)
  blocking collectives  201 us (18%)
  starting transfers between devices  35.8 us (3%)
  local copies, waits for them, and re-layouts  25 us (2%)
  matrix products  19.5 us (2%)
  between operations  18.4 us (2%)
  other arithmetic  16.8 us (1%)
    psum x1, waiting for transfers between devices, from_root(): return lax.psum(block, axis)  772 us
    all_gather x1, blocking collectives, on_device(): all_inverse = lax.all_gather(inverse, 'shard', axis=0, tiled=True)  193 us
    all_to_all x4, starting transfers between devices, on_device(): lax.all_to_all(own_rows, 'shard', split_axis=0, concat_axis=2, tiled=True)  35.4 us
    all_gather x4, waiting for transfers between devices, report_the_spots(): return all_gather(frame, axis_name='rep').sum(axis=0)  28.6 us
  transfers between devices with their start and end apart: 9, of which 5 were waited for; matrix products, arithmetic and copies ran while one was open for 3% of the time, Pallas kernels for 0%

profile of v1, /device:TPU:32, one launch (start us, length us, event | category | flops | bytes accessed | tf_op | source)
XLA Modules:
  0.0 1139.3 jit_solution(13977109982011696241)
XLA Ops:
  11.1 3.4 copy.8
  15.5 6.1 copy_bitcast_fusion.2
  21.6 6.0 copy_bitcast_fusion
  28.5 1.6 copy-done
  30.1 3.7 fusion
  33.8 771.8 %all-reduce.3.cloned.1.call-done = (bf16[256,4096]{1,0:T(8,128)(2,1)}, bf16[256,4096]{1,0:T(8,128)(2,1)}, bf16[256,4096]{1,0:T(8,128)(2,1)}, bf16[256,4096]{1,0:T(8,128)(2,1)}) async-done(((bf16[256,4096]{1,0:T(8,128)(2,1)}, bf16[256,4096]{1,0:T(8,128)(2,1)}, bf16[256,4096]{1,0:T(8,128)(2,1)}, bf16[256,4096]{1,0:T(8,128)(2,1)}), (bf16[256,4096]{1,0:T(8,128)(2,1)}, bf16[256,4096]{1,0:T(8,128)(2,1)}, ...) | async-done | bytes 8388624 | tf_op jit(solution)/shard_map/psum | solution.py:17
  805.6 5.1 fusion.4
  810.7 4.6 fusion.5
  815.4 5.1 fusion.6
  820.6 4.8 fusion.3
  825.4 7.9 psum.36
  833.3 7.6 all-gather.12.cloned.1.call-done
  840.9 1.9 reduce_sum.37
  843.7 13.1 %all-to-all-start.1 = ((f32[64,1,512]{2,1,0:T(1,128)}), f32[64,1,512]{2,1,0:T(1,128)S(1)}, u32[]{:S(2)}, u32[]{:S(2)}) async-start(f32[64,1,512]{2,1,0:T(1,128)} %dynamic-slice_bitcast_fusion.2), calls=%async_computation.1 | async-start | bytes 262144 | tf_op jit(solution)/shard_map/all_to_all | solution.py:57
  856.9 21.0 %all-gather.14.cloned.1.call-done = f32[1024,512]{1,0:T(8,128)} async-done(((f32[256,512]{1,0:T(8,128)}), f32[1024,512]{1,0:T(8,128)}) %all-gather.14.cloned.1.call-update) | async-done | bytes 2097168 | tf_op jit(solution)/shard_map/all_gather | solution.py:53
  877.8 1.9 reduce_sum.38
  880.6 12.9 %all-to-all-start.2 = ((f32[64,1,512]{2,1,0:T(1,128)}), f32[64,1,512]{2,1,0:T(1,128)S(1)}, u32[]{:S(2)}, u32[]{:S(2)}) async-start(f32[64,1,512]{2,1,0:T(1,128)} %dynamic-slice_bitcast_fusion.1), calls=%async_computation.2 | async-start | bytes 262144 | tf_op jit(solution)/shard_map/all_to_all | solution.py:57
  893.5 193.0 %all-gather.4 = f32[64,1,512]{2,1,0:T(1,128)S(1)} all-gather(f32[1,1,512]{2,1,0:T(1,128)S(1)} %bitcast.89), channel_id=1, replica_groups=mesh['shard'=64,'rep'=4] {'shard'}, dimensions={0}, use_global_device_ids=true | all-gather | bytes 133120 | tf_op jit(solution)/shard_map/all_gather | solution.py:36
  1090.9 1.9 reduce_sum.39
  1092.9 1.9 reduce_sum.36
  1095.7 4.8 all-to-all-start.3
  1102.1 11.1 all-to-all-done.3
  1113.2 4.6 all-to-all-start
  1119.1 11.3 all-to-all-done
  (50 shorter events, 13.9 us)
Async XLA Ops:
  6.5 799.0 %all-reduce.3.cloned.1.call-start = ((), (), s32[]{:S(2)}) async-start(), calls=%async_computation.8 | async-start | bytes 16777216 | tf_op jit(solution)/shard_map/psum | solution.py:17
  27.7 813.2 %all-gather.12.cloned.1.call-start = ((), (), s32[]{:S(2)}) async-start(), calls=%async_computation.5 | async-start | bytes 2621440 | tf_op jit(solution)/shard_map/all_gather | solution.py:53
  27.9 2.2 copy-start
  805.6 5.1 copy-start.2
  810.7 67.2 %all-gather.14.cloned.1.call-start = ((), (), s32[]{:S(2)}) async-start(), calls=%async_computation.6 | async-start | bytes 2621440 | tf_op jit(solution)/shard_map/all_gather | solution.py:53
  815.4 275.5 %all-gather.16.cloned.1.call-start = ((), (), s32[]{:S(2)}) async-start(), calls=%async_computation.7 | async-start | bytes 2621440 | tf_op jit(solution)/shard_map/all_gather | solution.py:53
  815.4 5.2 copy-start.1
  820.5 272.4 %all-gather.10.cloned.1.call-start = ((), (), s32[]{:S(2)}) async-start(), calls=%async_computation.4 | async-start | bytes 2621440 | tf_op jit(solution)/shard_map/all_gather | solution.py:53
  843.7 36.9 %all-to-all-start.1 = ((f32[64,1,512]{2,1,0:T(1,128)}), f32[64,1,512]{2,1,0:T(1,128)S(1)}, u32[]{:S(2)}, u32[]{:S(2)}) async-start(f32[64,1,512]{2,1,0:T(1,128)} %dynamic-slice_bitcast_fusion.2), calls=%async_computation.1 | async-start | bytes 262144 | tf_op jit(solution)/shard_map/all_to_all | solution.py:57
  880.6 215.1 %all-to-all-start.2 = ((f32[64,1,512]{2,1,0:T(1,128)}), f32[64,1,512]{2,1,0:T(1,128)S(1)}, u32[]{:S(2)}, u32[]{:S(2)}) async-start(f32[64,1,512]{2,1,0:T(1,128)} %dynamic-slice_bitcast_fusion.1), calls=%async_computation.2 | async-start | bytes 262144 | tf_op jit(solution)/shard_map/all_to_all | solution.py:57
  1095.7 17.4 %all-to-all-start.3 = ((f32[64,1,512]{2,1,0:T(1,128)}), f32[64,1,512]{2,1,0:T(1,128)S(1)}, u32[]{:S(2)}, u32[]{:S(2)}) async-start(f32[64,1,512]{2,1,0:T(1,128)} %dynamic-slice_bitcast_fusion), calls=%async_computation.3 | async-start | bytes 262144 | tf_op jit(solution)/shard_map/all_to_all | solution.py:57
  1113.2 17.2 %all-to-all-start = ((f32[64,1,512]{2,1,0:T(1,128)}), f32[64,1,512]{2,1,0:T(1,128)S(1)}, u32[]{:S(2)}, u32[]{:S(2)}) async-start(f32[64,1,512]{2,1,0:T(1,128)} %dynamic-slice_bitcast_fusion.3), calls=%async_computation | async-start | bytes 262144 | tf_op jit(solution)/shard_map/all_to_all | solution.py:57
Sparse Core Ops, SparseCore 0:
  27.8 777.7 all-reduce.2
  810.8 30.0 all-gather.11
  842.7 35.0 all-gather.13
  879.5 34.5 all-gather.15
  915.7 31.8 all-gather.9
